TPU v7x, 256 devices: a whole 4x4x8 slice. The times are simulated.
256 devices in a mesh: section: 16 (over y, x), dp: 16 (over z, core).
Axes of the slice: x: 4, y: 4, z: 8, core: 2. Of those that a mesh axis runs over, the one named last changes fastest.
Arguments:
- hidden: bfloat16 [16, 256, 8192], P('dp', 'section'), may hold values from -1500 to 1500
- head: bfloat16 [65536, 8192], P('section', 'dp'), may hold values from -0.0625 to 0.0625
- block_id: int32 [16, 16], P(None, 'section'), may hold values from 0 to 7
- block_live: int32 [16, 16], P(None, 'section'), may hold values from 0 to 1, as said below
- teacher: bfloat16 [16, 256, 8192], P('dp', None, 'section'), may hold values from -400 to 400
Outputs:
- grad_hidden: bfloat16 [16, 256, 8192], P('dp', 'section')
- grad_head: bfloat16 [65536, 8192], P('section', 'dp')
Inputs may be any that keep to these rules, and one draw needn't show every extreme that they name: `block_live`: every micro-batch has at least one live section.
All inputs are finite; a program needn't handle non-finite values.
Results may differ from a plain program's by a relative error of at most 0.0056.
Values may be sent and summed in bfloat16 or wider, within the bound.
No kernel may reach another device: no remote copies, remote signals or barrier semaphores. Data moves between devices by JAX's collectives and lax.ppermute only.
A program may use at most 128 MiB of HBM per device.

v0:
```python
import jax
import jax.numpy as jnp
from jax import lax
from jax.sharding import PartitionSpec as P

neg_fill = -1e30


def local(hidden, head, block_id, block_live, teacher):
    my_replica = lax.axis_index("dp")
    n_dp = lax.axis_size("dp")
    tok_local = hidden.shape[1]
    model_width = hidden.shape[2]
    block_rows = teacher.shape[2]
    col_width = head.shape[1]
    blocks = head.shape[0] // block_rows
    table = head.reshape(blocks, block_rows, col_width)
    block_ids = block_id[:, 0]
    live_flags = block_live[:, 0]
    n_mb = block_ids.shape[0]
    pieces = hidden.reshape(1, tok_local, n_dp, col_width)
    pieces = lax.all_to_all(pieces, "dp", split_axis=2, concat_axis=0, tiled=True)
    hid_w = lax.all_gather(pieces, "section", axis=1, tiled=True).reshape(n_mb, -1, col_width)
    picked = jnp.take(table, block_ids, axis=0)
    part = jnp.einsum("mtw,mrw->mtr", hid_w, picked, preferred_element_type=jnp.float32)
    logits = lax.psum_scatter(part, "dp", scatter_dimension=0, tiled=True)[0]
    own_live = lax.dynamic_index_in_dim(live_flags, my_replica, 0, keepdims=False) > 0
    teach = teacher[0].astype(jnp.float32)
    live_value = jnp.where(own_live, 1.0, 0.0).astype(jnp.float32)
    stud_local = jnp.where(own_live, jnp.max(logits, axis=1), neg_fill)
    teach_local = jnp.where(own_live, jnp.max(teach, axis=1), neg_fill)
    stud_top, teach_top = lax.pmax((stud_local, teach_local), "section")
    stud_part = jnp.where(own_live, jnp.sum(jnp.exp(logits - stud_top[:, None]), axis=1), 0.0)
    teach_part = jnp.where(own_live, jnp.sum(jnp.exp(teach - teach_top[:, None]), axis=1), 0.0)
    stud_total, teach_total, live_count = lax.psum((stud_part, teach_part, live_value), "section")
    student = jnp.where(own_live, jnp.exp(logits - stud_top[:, None]) / stud_total[:, None], 0.0)
    teach_prob = jnp.where(
        own_live, jnp.exp(teach - teach_top[:, None]) / teach_total[:, None], 0.0
    )
    logit_grad = (block_rows * live_count * (student - teach_prob)).astype(jnp.bfloat16)
    grads = lax.all_gather(logit_grad[None], "dp", axis=0, tiled=True)
    contrib = jnp.einsum("mtr,mtw->mrw", grads, hid_w, preferred_element_type=jnp.float32).astype(
        jnp.bfloat16
    )
    block_range = jnp.arange(blocks, dtype=jnp.int32)[None, :]
    selector = jnp.where(
        (live_flags[:, None] > 0) & (block_ids[:, None] == block_range), 1.0, 0.0
    ).astype(jnp.bfloat16)
    grad_head = jnp.einsum("mb,mrw->brw", selector, contrib, preferred_element_type=jnp.float32)
    grad_head = grad_head.astype(jnp.bfloat16).reshape(blocks * block_rows, col_width)
    ghid = jnp.einsum("mtr,mrw->mtw", grads, picked, preferred_element_type=jnp.float32)
    ghid = lax.psum_scatter(ghid, "section", scatter_dimension=1, tiled=True).astype(jnp.bfloat16)
    ghid = lax.all_to_all(ghid, "dp", split_axis=0, concat_axis=2, tiled=True)
    grad_hidden = ghid.reshape(1, tok_local, model_width)
    return (grad_hidden, grad_head)


def solution(mesh):
    placed = (
        P("dp", "section", None),
        P("section", "dp"),
        P(None, "section"),
        P(None, "section"),
        P("dp", None, "section"),
    )
    return jax.shard_map(
        local,
        mesh=mesh,
        in_specs=placed,
        out_specs=(P("dp", "section", None), P("section", "dp")),
        check_vma=False,
    )
```

profile of v0, /device:TPU:1, one launch (start us, length us, event | category | flops | bytes accessed | tf_op | source)
XLA Modules:
  0.0 412.9 jit_solution(15351352990721341709)
XLA Ops:
  7.2 1.0 copy.29
  8.2 21.6 %all_to_all.36 = bf16[1,16,16,512]{3,1,0,2:T(8,128)(2,1)} all-to-all(bf16[1,16,16,512]{3,1,0,2:T(8,128)(2,1)S(1)} %bitcast.54), channel_id=1, replica_groups=mesh['section'=16,'dp'=16] {'dp'}, dimensions={2} | all-to-all | bytes 524288 | tf_op jit(solution)/shard_map/all_to_all | solution.py:22
  29.8 0.0 reduce-scatter.3.cloned.1.call-start
  29.8 0.7 fusion.34
  30.5 7.0 %gather_fusion = bf16[16,512,512]{2,1,0:T(8,128)(2,1)} fusion(bf16[8,512,512]{2,1,0:T(8,128)(2,1)} %bitcast.50, s32[1024]{0:T(1024)S(1)} %pad_clamp_fusion), kind=kCustom, calls=%fused_computation | custom fusion | bytes 16777280 | tf_op jit(solution)/shard_map/jit(_take)/gather | solution.py:24
  37.5 45.8 %all-gather.6.cloned.1.call-done = bf16[16,1,256,1,512]{4,2,0,3,1:T(8,128)(2,1)} async-done(((bf16[16,1,16,1,512]{4,2,0,3,1:T(8,128)(2,1)}), bf16[16,1,256,1,512]{4,2,0,3,1:T(8,128)(2,1)}) %all-gather.6.cloned.1.call-update) | async-done | bytes 4194320 | tf_op jit(solution)/shard_map/all_gather | solution.py:23
  83.3 10.2 %fusion.6 = f32[16,256,512]{1,2,0:T(8,128)} fusion(bf16[16,1,256,1,512]{4,2,0,3,1:T(8,128)(2,1)} %all-gather.6.cloned.1.call-done, bf16[16,512,512]{2,1,0:T(8,128)(2,1)} %gather_fusion, pred[16]{0:T(512)(128)(4,1)S(1)} %and_bitcast_fusion), kind=kOutput, calls=%fused_computation.9 | convolution fusion | flops 2151677952 | bytes 20971536 | tf_op jit(solution)/shard_map/mtw,mrw->mtr/dot_general | solution.py:25
  93.5 0.9 copy-done
  94.4 0.1 copy.15
  94.6 0.1 reduce_max.24
  94.7 0.6 fusion.35
  95.9 0.6 convert_select_fusion
  96.6 64.4 %reduce-scatter.3.cloned.1.call-done = f32[1,256,512]{1,2,0:T(8,128)} async-done(((f32[16,256,512]{1,2,0:T(8,128)}), f32[1,256,512]{1,2,0:T(8,128)}) %reduce-scatter.3.cloned.1.call-update) | async-done | bytes 524304 | tf_op jit(solution)/shard_map/reduce_scatter | solution.py:26
  161.0 1.1 reduce_max.23
  162.1 0.6 broadcast_select_fusion.7
  162.8 33.3 %all-reduce.1 = (f32[256]{0:T(256)S(1)}, f32[256]{0:T(256)S(1)}) all-reduce(f32[256]{0:T(256)S(1)} %convert_select_fusion, f32[256]{0:T(256)S(1)} %broadcast_select_fusion.7), channel_id=1, replica_groups=mesh['section'=16,'dp'=16] {'section'}, use_global_device_ids=true, to_apply=%region_7.8 | all-reduce | flops 512 | bytes 4096 | tf_op jit(solution)/shard_map/pmax | solution.py:32
  196.1 0.1 fusion.19
  196.2 1.2 fusion.21
  197.4 0.6 broadcast_select_fusion.5
  198.0 29.2 %all-reduce = (f32[256]{0:T(256)S(1)}, f32[256]{0:T(256)S(1)}, f32[]{:T(128)}) all-reduce(f32[256]{0:T(256)S(1)} %get-tuple-element.7, f32[256]{0:T(256)S(1)} %get-tuple-element.8, f32[]{:T(128)S(6)} %select_n.58), channel_id=1, replica_groups=mesh['section'=16,'dp'=16] {'section'}, use_global_device_ids=true, to_apply=%region_9.10 | all-reduce | flops 513 | bytes 4104 | tf_op jit(solution)/shard_map/psum | solution.py:35
  227.9 1.9 fusion.22
  229.8 0.8 copy.16
  230.7 54.8 %all-gather.4.cloned.1.call-done = bf16[16,256,512]{2,1,0:T(8,128)(2,1)} async-done(((bf16[1,256,512]{2,1,0:T(8,128)(2,1)}), bf16[16,256,512]{2,1,0:T(8,128)(2,1)}) %all-gather.4.cloned.1.call-update) | async-done | bytes 4194320 | tf_op jit(solution)/shard_map/all_gather | solution.py:41
  285.5 10.3 %fusion.5 = f32[16,256,512]{2,1,0:T(8,128)} fusion(bf16[16,256,512]{2,1,0:T(8,128)(2,1)} %all-gather.4.cloned.1.call-done, bf16[16,512,512]{2,1,0:T(8,128)(2,1)} %gather_fusion, pred[16]{0:T(512)(128)(4,1)S(1)} %and_bitcast_fusion), kind=kOutput, calls=%fused_computation.8 | convolution fusion | flops 2151677952 | bytes 20971536 | tf_op jit(solution)/shard_map/mtr,mrw->mtw/dot_general | solution.py:51
  295.8 9.1 %convolution_convert_fusion = bf16[16,512,512]{2,1,0:T(8,128)(2,1)} fusion(bf16[16,256,512]{2,1,0:T(8,128)(2,1)} %all-gather.4.cloned.1.call-done, bf16[16,1,256,1,512]{4,2,0,3,1:T(8,128)(2,1)} %all-gather.6.cloned.1.call-done), kind=kOutput, calls=%fused_computation.4 | convolution fusion | flops 2151677952 | bytes 16777216 | tf_op jit(solution)/shard_map/mtr,mtw->mrw/dot_general | solution.py:42
  304.9 78.3 %reduce-scatter.5.cloned.1.call-done = f32[16,16,512]{2,1,0:T(8,128)} async-done(((f32[16,256,512]{2,1,0:T(8,128)}), f32[16,16,512]{2,1,0:T(8,128)}) %reduce-scatter.5.cloned.1.call-update) | async-done | bytes 524304 | tf_op jit(solution)/shard_map/reduce_scatter | solution.py:52
  383.2 1.8 convert_element_type.29
  385.0 9.0 %all-to-all-start.1 = ((bf16[16,16,512]{2,1,0:T(8,128)(2,1)}), bf16[16,16,512]{2,1,0:T(8,128)(2,1)S(1)}, u32[]{:S(2)}, u32[]{:S(2)}) async-start(bf16[16,16,512]{2,1,0:T(8,128)(2,1)} %convert_element_type.29), calls=%async_computation.3 | async-start | bytes 524288 | tf_op jit(solution)/shard_map/all_to_all | solution.py:53
  393.9 8.1 %fusion.9 = bf16[8,512,512]{2,0,1:T(8,128)(2,1)S(1)} fusion(bf16[16,512,512]{2,1,0:T(8,128)(2,1)} %convolution_convert_fusion, s32[16]{0:T(128)S(1)} %bitcast.57, pred[16]{0:T(512)(128)(4,1)S(1)} %compare_bitcast_fusion), kind=kOutput, calls=%fused_computation.10 | convolution fusion | flops 69206528 | bytes 12582992 | tf_op jit(solution)/shard_map/mb,mrw->brw/dot_general | solution.py:49
  402.0 3.5 copy.20
  405.5 0.1 all-to-all-done.1
  405.6 0.7 copy.23
  (15 shorter events, 0.2 us)
Async XLA Ops:
  7.2 76.1 %all-gather.6.cloned.1.call-start = ((), (), s32[]{:S(2)}) async-start(), calls=%async_computation.7 | async-start | bytes 4456448 | tf_op jit(solution)/shard_map/all_gather | solution.py:23
  29.8 131.2 %reduce-scatter.3.cloned.1.call-start = ((), (), s32[]{:S(2)}) async-start(), calls=%async_computation.4 | async-start | bytes 8912896 | tf_op jit(solution)/shard_map/reduce_scatter | solution.py:26
  30.5 7.0 %copy-start.1 = (s32[16,1]{0,1:T(1,128)S(1)}, s32[16,1]{0,1:T(1,128)}, u32[]{:S(2)}) copy-start(s32[16,1]{0,1:T(1,128)} %param.7) | copy-start | bytes 196
  93.5 0.9 copy-start
  93.5 1.2 copy-start.2
  93.5 192.0 %all-gather.4.cloned.1.call-start = ((), (), s32[]{:S(2)}) async-start(), calls=%async_computation.5 | async-start | bytes 4456448 | tf_op jit(solution)/shard_map/all_gather | solution.py:41
  230.7 152.5 %reduce-scatter.5.cloned.1.call-start = ((), (), s32[]{:S(2)}) async-start(), calls=%async_computation.6 | async-start | bytes 8912896 | tf_op jit(solution)/shard_map/reduce_scatter | solution.py:52
  385.0 20.7 %all-to-all-start.1 = ((bf16[16,16,512]{2,1,0:T(8,128)(2,1)}), bf16[16,16,512]{2,1,0:T(8,128)(2,1)S(1)}, u32[]{:S(2)}, u32[]{:S(2)}) async-start(bf16[16,16,512]{2,1,0:T(8,128)(2,1)} %convert_element_type.29), calls=%async_computation.3 | async-start | bytes 524288 | tf_op jit(solution)/shard_map/all_to_all | solution.py:53
Sparse Core Ops, SparseCore 0:
  29.9 53.3 all-gather.5
  93.6 67.3 reduce-scatter.2
  230.8 54.6 all-gather.3
  295.9 87.1 reduce-scatter.4
where the time goes:
time: 413 us
  waiting for transfers between devices  243 us (59%)
  blocking collectives  84.1 us (20%)
  matrix products  37.7 us (9%)
  between operations  15.1 us (4%)
  local copies, waits for them, and re-layouts  14 us (3%)
  other arithmetic  9.45 us (2%)
  starting transfers between devices  9.12 us (2%)
    reduce_scatter x1, waiting for transfers between devices, local(): lax.psum_scatter(ghid, 'section', scatter_dimension=1, tiled=True)  78.3 us
    reduce_scatter x1, waiting for transfers between devices, local(): logits = lax.psum_scatter(part, 'dp', scatter_dimension=0, tiled=True)[0]  64.4 us
    all_gather x1, waiting for transfers between devices, local(): grads = lax.all_gather(logit_grad[None], 'dp', axis=0, tiled=True)  54.8 us
    all_gather x1, waiting for transfers between devices, local(): lax.all_gather(pieces, 'section', axis=1, tiled=True)  45.8 us
    pmax x1, blocking collectives, local(): stud_top, teach_top = lax.pmax((stud_local, teach_local), 'section')  33.3 us
    psum x1, blocking collectives, local(): lax.psum((stud_part, teach_part, live_value), 'section')  29.2 us
    all_to_all x1, blocking collectives, local(): lax.all_to_all(pieces, 'dp', split_axis=2, concat_axis=0, tiled=True)  21.6 us
    dot_general x1, matrix products, local(): jnp.einsum('mtr,mrw->mtw', grads, picked, preferred_element_type=jnp.floa...  10.3 us
  transfers between devices with their start and end apart: 5, of which 5 were waited for; matrix products, arithmetic and copies ran while one was open for 7% of the time, Pallas kernels for 0%

commit v1 on v0

--- a/solution.py
+++ b/solution.py
@@ -4,6 +4,15 @@
 from jax.sharding import PartitionSpec as P
 
 neg_fill = -1e30
+
+
+def save_target(mat):
+    group_axis = "section"
+    cores_n = lax.axis_size(group_axis)
+    ledger = [cores_n if nth == 1 else 1 for nth in range(mat.ndim)]
+    return lax.all_to_all(
+        jnp.tile(mat, ledger), group_axis, split_axis=1, concat_axis=1, tiled=True
+    )
 
 
 def local(hidden, head, block_id, block_live, teacher):
@@ -20,7 +29,7 @@
     n_mb = block_ids.shape[0]
     pieces = hidden.reshape(1, tok_local, n_dp, col_width)
     pieces = lax.all_to_all(pieces, "dp", split_axis=2, concat_axis=0, tiled=True)
-    hid_w = lax.all_gather(pieces, "section", axis=1, tiled=True).reshape(n_mb, -1, col_width)
+    hid_w = save_target(pieces).reshape(n_mb, -1, col_width)
     picked = jnp.take(table, block_ids, axis=0)
     part = jnp.einsum("mtw,mrw->mtr", hid_w, picked, preferred_element_type=jnp.float32)
     logits = lax.psum_scatter(part, "dp", scatter_dimension=0, tiled=True)[0]

time: 413 us -> 429 us (1.039)
  starting transfers between devices: 9.12 us -> 16 us
    all_to_all x0 -> x1, waiting for transfers between devices: none -> 58.4 us  [save_target(): lax.all_to_all(jnp.tile(mat, ledger), group_axis, split_axis=1, concat_ax...]
    all_gather x1 -> x0, waiting for transfers between devices: 45.8 us -> none  [local(): lax.all_gather(pieces, 'section', axis=1, tiled=True)]
    all_to_all x0 -> x1, starting transfers between devices: none -> 6.81 us  [save_target(): lax.all_to_all(jnp.tile(mat, ledger), group_axis, split_axis=1, concat_ax...]
    reduce_scatter x1, waiting for transfers between devices: 64.4 us -> 57.8 us  [local(): logits = lax.psum_scatter(part, 'dp', scatter_dimension=0, tiled=True)[0]]
  transfers between devices with their start and end apart: 5 -> 5, of which waited for: 5 -> 5; matrix products, arithmetic and copies ran while one was open for 7% -> 8% of each run, Pallas kernels for 0% -> 0%
where the time goes in v1:
time: 429 us; the launch traced here: 428 us
  waiting for transfers between devices  246 us (57%)
  blocking collectives  84 us (20%)
  matrix products  41.8 us (10%)
  local copies, waits for them, and re-layouts  16.7 us (4%)
  starting transfers between devices  16 us (4%)
  between operations  15.2 us (4%)
  other arithmetic  8.79 us (2%)
    reduce_scatter x1, waiting for transfers between devices, local(): lax.psum_scatter(ghid, 'section', scatter_dimension=1, tiled=True)  74.9 us
    all_to_all x1, waiting for transfers between devices, save_target(): lax.all_to_all(jnp.tile(mat, ledger), group_axis, split_axis=1, concat_ax...  58.4 us
    reduce_scatter x1, waiting for transfers between devices, local(): logits = lax.psum_scatter(part, 'dp', scatter_dimension=0, tiled=True)[0]  57.8 us
    all_gather x1, waiting for transfers between devices, local(): grads = lax.all_gather(logit_grad[None], 'dp', axis=0, tiled=True)  54.7 us
    pmax x1, blocking collectives, local(): stud_top, teach_top = lax.pmax((stud_local, teach_local), 'section')  33.3 us
    psum x1, blocking collectives, local(): lax.psum((stud_part, teach_part, live_value), 'section')  29.2 us
    all_to_all x1, blocking collectives, local(): lax.all_to_all(pieces, 'dp', split_axis=2, concat_axis=0, tiled=True)  21.5 us
    dot_general x1, matrix products, local(): jnp.einsum('mtr,mtw->mrw', grads, hid_w, preferred_element_type=jnp.float32)  12.2 us
  transfers between devices with their start and end apart: 5, of which 5 were waited for; matrix products, arithmetic and copies ran while one was open for 8% of the time, Pallas kernels for 0%

profile of v1, /device:TPU:1, one launch (start us, length us, event | category | flops | bytes accessed | tf_op | source)
XLA Modules:
  0.0 428.3 jit_solution(14484752332999200372)
XLA Ops:
  7.2 1.0 copy.50
  8.2 21.5 %all_to_all.38 = bf16[1,16,16,512]{3,1,0,2:T(8,128)(2,1)S(1)} all-to-all(bf16[1,16,16,512]{3,1,0,2:T(8,128)(2,1)S(1)} %bitcast.58), channel_id=1, replica_groups=mesh['section'=16,'dp'=16] {'dp'}, dimensions={2} | all-to-all | bytes 524288 | tf_op jit(solution)/shard_map/all_to_all | solution.py:31
  29.6 0.1 copy.24
  29.8 2.5 tile.12
  32.3 6.8 %all-to-all-start.1 = ((bf16[16,256,1,512]{3,0,2,1:T(8,128)(2,1)}), bf16[16,256,1,512]{3,0,2,1:T(8,128)(2,1)}, u32[]{:S(2)}, u32[]{:S(2)}) async-start(bf16[16,256,1,512]{3,0,2,1:T(8,128)(2,1)} %bitcast.54), calls=%async_computation.1 | async-start | bytes 8388608 | tf_op jit(solution)/shard_map/all_to_all | solution.py:13
  39.2 7.0 %gather_fusion = bf16[16,512,512]{2,1,0:T(8,128)(2,1)} fusion(bf16[8,512,512]{2,1,0:T(8,128)(2,1)} %bitcast.53, s32[1024]{0:T(1024)S(1)} %pad_clamp_fusion), kind=kCustom, calls=%fused_computation | custom fusion | bytes 16777280 | tf_op jit(solution)/shard_map/jit(_take)/gather | solution.py:33
  46.2 58.4 %all-to-all-done.1 = bf16[16,256,1,512]{3,0,2,1:T(8,128)(2,1)} async-done(((bf16[16,256,1,512]{3,0,2,1:T(8,128)(2,1)}), bf16[16,256,1,512]{3,0,2,1:T(8,128)(2,1)}, u32[]{:S(2)}, u32[]{:S(2)}) %all-to-all-start.1) | async-done | bytes 4194336 | tf_op jit(solution)/shard_map/all_to_all | solution.py:13
  104.6 11.1 %fusion.8 = f32[16,256,512]{1,2,0:T(8,128)} fusion(bf16[16,256,1,512]{3,0,2,1:T(8,128)(2,1)} %all-to-all-done.1, bf16[16,512,512]{2,1,0:T(8,128)(2,1)} %gather_fusion, pred[16]{0:T(512)(128)(4,1)S(1)} %and_bitcast_fusion), kind=kOutput, calls=%fused_computation.11 | convolution fusion | flops 2151677952 | bytes 20971536 | tf_op jit(solution)/shard_map/mtw,mrw->mtr/dot_general | solution.py:34
  115.8 0.9 copy-done
  116.7 0.1 copy.26
  116.9 0.6 fusion.37
  118.2 0.6 convert_select_fusion
  118.8 57.8 %reduce-scatter.3.cloned.1.call-done = f32[1,256,512]{1,2,0:T(8,128)} async-done(((f32[16,256,512]{1,2,0:T(8,128)}), f32[1,256,512]{1,2,0:T(8,128)}) %reduce-scatter.3.cloned.1.call-update) | async-done | bytes 524304 | tf_op jit(solution)/shard_map/reduce_scatter | solution.py:35
  176.6 1.1 reduce_max.23
  177.7 0.6 broadcast_select_fusion.7
  178.4 33.3 %all-reduce.1 = (f32[256]{0:T(256)S(1)}, f32[256]{0:T(256)S(1)}) all-reduce(f32[256]{0:T(256)S(1)} %convert_select_fusion, f32[256]{0:T(256)S(1)} %broadcast_select_fusion.7), channel_id=1, replica_groups=mesh['section'=16,'dp'=16] {'section'}, use_global_device_ids=true, to_apply=%region_7.8 | all-reduce | flops 512 | bytes 4096 | tf_op jit(solution)/shard_map/pmax | solution.py:41
  211.8 1.2 fusion.23
  212.9 0.6 broadcast_select_fusion.5
  213.6 29.2 %all-reduce = (f32[256]{0:T(256)S(1)}, f32[256]{0:T(256)S(1)}, f32[]{:T(128)}) all-reduce(f32[256]{0:T(256)S(1)} %get-tuple-element.7, f32[256]{0:T(256)S(1)} %get-tuple-element.8, f32[]{:T(128)S(6)} %select_n.58), channel_id=1, replica_groups=mesh['section'=16,'dp'=16] {'section'}, use_global_device_ids=true, to_apply=%region_9.10 | all-reduce | flops 513 | bytes 4104 | tf_op jit(solution)/shard_map/psum | solution.py:44
  243.5 1.9 fusion.24
  245.4 0.8 copy.27
  246.3 0.2 reduce-scatter.5.cloned.1.call-start
  246.5 54.7 %all-gather.2.cloned.1.call-done = bf16[16,256,512]{2,1,0:T(8,128)(2,1)} async-done(((bf16[1,256,512]{2,1,0:T(8,128)(2,1)}), bf16[16,256,512]{2,1,0:T(8,128)(2,1)}) %all-gather.2.cloned.1.call-update) | async-done | bytes 4194320 | tf_op jit(solution)/shard_map/all_gather | solution.py:50
  301.2 10.3 %fusion.7 = f32[16,256,512]{2,1,0:T(8,128)} fusion(bf16[16,256,512]{2,1,0:T(8,128)(2,1)} %all-gather.2.cloned.1.call-done, bf16[16,512,512]{2,1,0:T(8,128)(2,1)} %gather_fusion, pred[16]{0:T(512)(128)(4,1)S(1)} %and_bitcast_fusion), kind=kOutput, calls=%fused_computation.10 | convolution fusion | flops 2151677952 | bytes 20971536 | tf_op jit(solution)/shard_map/mtr,mrw->mtw/dot_general | solution.py:60
  311.5 12.2 %convolution_convert_fusion = bf16[16,512,512]{2,1,0:T(8,128)(2,1)} fusion(bf16[16,256,512]{2,1,0:T(8,128)(2,1)} %all-gather.2.cloned.1.call-done, bf16[16,256,1,512]{3,0,2,1:T(8,128)(2,1)} %all-to-all-done.1), kind=kOutput, calls=%fused_computation.4 | convolution fusion | flops 2151677952 | bytes 16777216 | tf_op jit(solution)/shard_map/mtr,mtw->mrw/dot_general | solution.py:51
  323.7 74.9 %reduce-scatter.5.cloned.1.call-done = f32[16,16,512]{2,1,0:T(8,128)} async-done(((f32[16,256,512]{2,1,0:T(8,128)}), f32[16,16,512]{2,1,0:T(8,128)}) %reduce-scatter.5.cloned.1.call-update) | async-done | bytes 524304 | tf_op jit(solution)/shard_map/reduce_scatter | solution.py:61
  398.6 1.8 convert_element_type.29
  400.4 8.9 %all-to-all-start.2 = ((bf16[16,16,512]{2,1,0:T(8,128)(2,1)}), bf16[16,16,512]{2,1,0:T(8,128)(2,1)S(1)}, u32[]{:S(2)}, u32[]{:S(2)}) async-start(bf16[16,16,512]{2,1,0:T(8,128)(2,1)} %convert_element_type.29), calls=%async_computation.4 | async-start | bytes 524288 | tf_op jit(solution)/shard_map/all_to_all | solution.py:62
  409.3 8.1 %fusion.11 = bf16[8,512,512]{2,0,1:T(8,128)(2,1)S(1)} fusion(bf16[16,512,512]{2,1,0:T(8,128)(2,1)} %convolution_convert_fusion, s32[16]{0:T(128)S(1)} %bitcast.61, pred[16]{0:T(512)(128)(4,1)S(1)} %compare_bitcast_fusion), kind=kOutput, calls=%fused_computation.12 | convolution fusion | flops 69206528 | bytes 12582992 | tf_op jit(solution)/shard_map/mb,mrw->brw/dot_general | solution.py:58
  417.4 3.5 copy.31
  420.9 0.1 all-to-all-done.2
  421.0 0.7 copy.34
  (16 shorter events, 0.4 us)
Async XLA Ops:
  7.2 32.0 %copy-start.1 = (s32[16,1]{0,1:T(1,128)S(1)}, s32[16,1]{0,1:T(1,128)}, u32[]{:S(2)}) copy-start(s32[16,1]{0,1:T(1,128)} %param.7) | copy-start | bytes 196
  32.3 72.2 %all-to-all-start.1 = ((bf16[16,256,1,512]{3,0,2,1:T(8,128)(2,1)}), bf16[16,256,1,512]{3,0,2,1:T(8,128)(2,1)}, u32[]{:S(2)}, u32[]{:S(2)}) async-start(bf16[16,256,1,512]{3,0,2,1:T(8,128)(2,1)} %bitcast.54), calls=%async_computation.1 | async-start | bytes 8388608 | tf_op jit(solution)/shard_map/all_to_all | solution.py:13
  39.2 137.5 %reduce-scatter.3.cloned.1.call-start = ((), (), s32[]{:S(2)}) async-start(), calls=%async_computation.5 | async-start | bytes 8912896 | tf_op jit(solution)/shard_map/reduce_scatter | solution.py:35
  115.7 0.9 copy-start
  115.7 1.2 copy-start.2
  115.7 185.4 %all-gather.2.cloned.1.call-start = ((), (), s32[]{:S(2)}) async-start(), calls=%async_computation.6 | async-start | bytes 4456448 | tf_op jit(solution)/shard_map/all_gather | solution.py:50
  246.3 152.4 %reduce-scatter.5.cloned.1.call-start = ((), (), s32[]{:S(2)}) async-start(), calls=%async_computation.7 | async-start | bytes 8912896 | tf_op jit(solution)/shard_map/reduce_scatter | solution.py:61
  400.4 20.6 %all-to-all-start.2 = ((bf16[16,16,512]{2,1,0:T(8,128)(2,1)}), bf16[16,16,512]{2,1,0:T(8,128)(2,1)S(1)}, u32[]{:S(2)}, u32[]{:S(2)}) async-start(bf16[16,16,512]{2,1,0:T(8,128)(2,1)} %convert_element_type.29), calls=%async_computation.4 | async-start | bytes 524288 | tf_op jit(solution)/shard_map/all_to_all | solution.py:62
Sparse Core Ops, SparseCore 0:
  115.9 60.6 reduce-scatter.2
  246.4 54.7 all-gather.1
  311.6 86.9 reduce-scatter.4
